TPU v7x, 32 devices: a whole 2x2x4 slice. The times are simulated.
32 devices in a mesh: pair: 8 (over z, y), virt: 4 (over x, core).
Axes of the slice: x: 2, y: 2, z: 4, core: 2. Of those that a mesh axis runs over, the one named last changes fastest.
Arguments:
- amps_pm: bfloat16 [64, 64, 4096], P(('pair', 'virt')), may hold values from -6 to 6
- integrals: bfloat16 [32, 4096, 2048], P(('pair', 'virt')), may hold values from -0.046875 to 0.046875
- fock_vv: bfloat16 [512, 512], replicated, may hold values from -0.25 to 0.25
- blk_tiles: int32 [32, 2], replicated, may hold values from 0 to 63, as said below
- blk_mask: int32 [32], replicated, may hold values 0 or 1
Outputs:
- sigma: bfloat16 [64, 64, 2048], P('pair', 'virt')
Inputs may be any that keep to these rules, and one draw needn't show every extreme that they name: Each row is (input tile pair, output tile pair). Integral tile r belongs to device r // 1 of the joined axis pair+virt, and its input tile pair lies in that device's virt slab: blk_tiles[r, 0] // 16 == (r) % 4. No two rows are equal.
All inputs are finite; a program needn't handle non-finite values.
Results may differ from a plain program's by a relative error of at most 0.0033.
Values may be sent and summed in bfloat16 or wider, within the bound.
No kernel may reach another device: no remote copies, remote signals or barrier semaphores. Data moves between devices by JAX's collectives and lax.ppermute only.
A program may use at most 128 MiB of HBM per device.

v0:
```python
import jax
import jax.numpy as jnp
from jax import lax
from jax.sharding import PartitionSpec as P

TILE = 64
NVT = 8
A_W = 8
AS = 32


def per_device(amps_pm, integrals, fock_vv, blk_tiles, blk_mask):
    n_virt = lax.axis_size("virt")
    n_pair = lax.axis_size("pair")
    pm_rows, n_tiles, tile_len = amps_pm.shape
    blk_dev = integrals.shape[0]
    out_cols = integrals.shape[2]
    slab = n_tiles // n_virt
    device = lax.axis_index(("pair", "virt"))
    virt_idx = lax.axis_index("virt")
    own_tiles = lax.dynamic_slice_in_dim(blk_tiles, device * blk_dev, blk_dev, 0)
    own_mask = lax.dynamic_slice_in_dim(blk_mask, device * blk_dev, blk_dev, 0).astype(jnp.float32)
    local_in = own_tiles[:, 0] - virt_idx * slab
    amps_vm = lax.all_to_all(amps_pm, "virt", split_axis=1, concat_axis=0, tiled=True)
    sub_rows = amps_pm[:, :, :out_cols].reshape(pm_rows, A_W, NVT, AS, TILE)
    fock_four = fock_vv.reshape(NVT, TILE, NVT, TILE)
    onebody = jnp.einsum(
        "pkqsd,bjqd->pkbsj", sub_rows, fock_four, preferred_element_type=jnp.float32
    )
    onebody = onebody.reshape(pm_rows, n_tiles, out_cols)
    arrived = lax.all_to_all(onebody, "virt", split_axis=1, concat_axis=0, tiled=True)
    chosen = jnp.take(lax.all_gather(amps_vm, "pair", axis=0, tiled=True), local_in, axis=1)
    product = jnp.einsum("rkc,kco->rko", chosen, integrals, preferred_element_type=jnp.float32)
    partial_value = product * own_mask[None, :, None]
    p_dev = partial_value.shape[0] // n_pair
    dest_virt = own_tiles[:, 1] // slab
    virt_ids = jnp.arange(n_virt, dtype=jnp.int32)
    select = (virt_ids[:, None] == dest_virt[None, :]).astype(jnp.float32)
    outgoing = (
        partial_value.reshape(n_pair, 1, p_dev, blk_dev, out_cols) * select[None, :, None, :, None]
    )
    outgoing = outgoing.reshape(n_pair * n_virt * p_dev, blk_dev, out_cols)
    received = lax.all_to_all(
        outgoing.astype(jnp.bfloat16), ("pair", "virt"), split_axis=0, concat_axis=1, tiled=True
    ).astype(outgoing.dtype)
    my_tiles = virt_idx * slab + jnp.arange(slab, dtype=jnp.int32)
    one_hot = (blk_tiles[:, 1][:, None] == my_tiles[None, :]).astype(jnp.float32)
    summed = jnp.einsum("pro,rt->pto", received, one_hot, precision=lax.Precision.HIGHEST)
    return (summed + arrived).astype(jnp.bfloat16)


def solution(mesh):
    return jax.shard_map(
        per_device,
        mesh=mesh,
        in_specs=(P(("pair", "virt"), None, None), P(("pair", "virt"), None, None), P(), P(), P()),
        out_specs=P("pair", "virt", None),
        check_vma=False,
    )
```

profile of v0, /device:TPU:0, one launch (start us, length us, event | category | flops | bytes accessed | tf_op | source)
XLA Modules:
  0.0 224.9 jit_solution(6049675598253406029)
XLA Ops:
  6.5 2.3 %copy.16 = bf16[2,64,4096]{2,0,1:T(2,128)(2,1)S(1)} copy(bf16[2,64,4096]{2,1,0:T(8,128)(2,1)} %param.5) | data formatting | bytes 2097152 | tf_op args[0]
  8.9 18.5 %all_to_all.54 = bf16[2,64,4096]{2,0,1:T(2,128)(2,1)S(1)} all-to-all(bf16[2,64,4096]{2,0,1:T(2,128)(2,1)S(1)} %copy.16), channel_id=1, replica_groups=mesh['pair'=8,'virt'=4] {'virt'}, dimensions={1} | all-to-all | bytes 2097152 | tf_op jit(solution)/shard_map/all_to_all | solution.py:24
  27.3 0.6 copy.17
  27.9 1.0 copy.18
  29.0 0.1 slice-done
  29.1 1.1 reshape.154
  30.2 0.5 reshape.111
  30.7 1.3 convolution_bitcast_fusion.1
  32.0 0.2 copy.30
  32.2 2.1 reshape.157
  34.3 3.5 %all-to-all-start.2 = ((f32[2,64,2048]{2,0,1:T(2,128)}), f32[2,64,2048]{2,0,1:T(2,128)S(1)}, u32[]{:S(2)}, u32[]{:S(2)}) async-start(f32[2,64,2048]{2,0,1:T(2,128)} %reshape.157), calls=%async_computation.2 | async-start | bytes 2097152 | tf_op jit(solution)/shard_map/all_to_all | solution.py:31
  37.9 0.1 constant_dynamic-slice_fusion.1
  38.0 0.5 fusion.22
  41.1 0.6 dynamic_slice.7
  43.1 0.1 mul.69
  43.2 110.7 %all-gather.2.cloned.1.call-done = bf16[64,16,4096]{2,1,0:T(8,128)(2,1)} async-done(((bf16[8,16,4096]{2,1,0:T(8,128)(2,1)}), bf16[64,16,4096]{2,1,0:T(8,128)(2,1)}) %all-gather.2.cloned.1.call-update) | async-done | bytes 8388624 | tf_op jit(solution)/shard_map/all_gather | solution.py:32
  153.9 3.5 %constant_dynamic-slice_fusion = bf16[64,1,4096]{2,1,0:T(2,128)(2,1)S(1)} fusion(bf16[64,16,4096]{2,1,0:T(8,128)(2,1)} %all-gather.2.cloned.1.call-done, s32[]{:T(128)} %bitcast.8), kind=kLoop, calls=%fused_computation.22 | loop fusion | bytes 1048580 | solution.py:32
  157.5 9.2 %fusion.7 = f32[8,8,2048]{2,1,0:T(8,128)S(1)} fusion(bf16[1,4096,2048]{2,1,0:T(8,128)(2,1)} %param.6, bf16[64,1,4096]{2,1,0:T(2,128)(2,1)S(1)} %constant_dynamic-slice_fusion, pred[]{:T(512)} %bitcast.4, f32[]{:T(128)} %bitcast.11), kind=kOutput, calls=%fused_computation.6 | convolution fusion | flops 1074135040 | bytes 17825796 | tf_op jit(solution)/shard_map/rkc,kco->rko/dot_general | solution.py:33
  166.6 0.2 mul.66
  166.9 3.5 %mul.67 = f32[256,1,2048]{2,1,0:T(1,128)} reshape(f32[8,4,8,2048]{3,2,1,0:T(8,128)S(1)} %mul.66) | data formatting | bytes 4194304 | tf_op jit(solution)/shard_map/mul | solution.py:40
  170.4 3.1 %multiply_convert_fusion = bf16[256,1,2048]{2,1,0:T(2,128)(2,1)S(1)} fusion(f32[256,1,2048]{2,1,0:T(1,128)} %mul.67, f32[256]{0:T(256)S(1)} %mul.69), kind=kLoop, calls=%fused_computation.7 | loop fusion | flops 1048576 | bytes 3146752 | tf_op jit(solution)/shard_map/convert_element_type | solution.py:44
  173.5 0.5 broadcast.110
  174.0 7.8 %reduce = bf16[256,2048]{1,0:T(8,128)(2,1)} reduce(bf16[256,1,2048]{2,1,0:T(2,128)(2,1)S(1)} %multiply_convert_fusion, bf16[]{:T(256)} %broadcast.110), dimensions={1}, to_apply=%multiply_convert_fusion.reduce_sub_computation | reduce | bytes 2097154 | tf_op jit(solution)/shard_map/convert_element_type | solution.py:44
  181.8 2.9 %reshape.158 = bf16[32,2,8192]{2,1,0:T(2,128)(2,1)} reshape(bf16[256,2048]{1,0:T(8,128)(2,1)} %reduce) | data formatting | bytes 2097152
  184.7 2.8 %all-to-all-start.1 = ((bf16[32,2,8192]{2,1,0:T(2,128)(2,1)}), bf16[32,2,8192]{2,1,0:T(2,128)(2,1)S(1)}, u32[]{:S(2)}, u32[]{:S(2)}) async-start(bf16[32,2,8192]{2,1,0:T(2,128)(2,1)} %reshape.158), calls=%async_computation.1 | async-start | bytes 2097152 | tf_op jit(solution)/shard_map/all_to_all | solution.py:43
  187.6 0.6 copy.24
  188.2 1.1 copy.25
  189.3 24.5 %all-to-all-done.1 = bf16[32,2,8192]{2,1,0:T(2,128)(2,1)S(1)} async-done(((bf16[32,2,8192]{2,1,0:T(2,128)(2,1)}), bf16[32,2,8192]{2,1,0:T(2,128)(2,1)S(1)}, u32[]{:S(2)}, u32[]{:S(2)}) %all-to-all-start.1) | async-done | bytes 1048608 | tf_op jit(solution)/shard_map/all_to_all | solution.py:43
  213.7 1.0 reshape.159
  214.8 0.6 copy.45
  215.4 0.6 copy-done
  216.0 2.0 fusion.3
  (15 shorter events, 0.1 us)
Async XLA Ops:
  6.5 147.4 %all-gather.2.cloned.1.call-start = ((), (), s32[]{:S(2)}) async-start(), calls=%async_computation.3 | async-start | bytes 9437184 | tf_op jit(solution)/shard_map/all_gather | solution.py:32
  27.9 1.2 slice-start
  28.9 1.2 copy-start.1
  32.2 5.7 %copy-start.2 = (s32[32,2]{0,1:T(2,128)S(1)}, s32[32,2]{0,1:T(2,128)}, u32[]{:S(2)}) copy-start(s32[32,2]{0,1:T(2,128)} %param.8) | copy-start | bytes 772
  32.2 8.9 %copy-start.3 = (s32[32]{0:T(128)S(1)}, s32[32]{0:T(128)}, u32[]{:S(2)}) copy-start(s32[32]{0:T(128)} %param.9) | copy-start | bytes 388
  34.3 150.4 %all-to-all-start.2 = ((f32[2,64,2048]{2,0,1:T(2,128)}), f32[2,64,2048]{2,0,1:T(2,128)S(1)}, u32[]{:S(2)}, u32[]{:S(2)}) async-start(f32[2,64,2048]{2,0,1:T(2,128)} %reshape.157), calls=%async_computation.2 | async-start | bytes 2097152 | tf_op jit(solution)/shard_map/all_to_all | solution.py:31
  184.7 29.0 %all-to-all-start.1 = ((bf16[32,2,8192]{2,1,0:T(2,128)(2,1)}), bf16[32,2,8192]{2,1,0:T(2,128)(2,1)S(1)}, u32[]{:S(2)}, u32[]{:S(2)}) async-start(bf16[32,2,8192]{2,1,0:T(2,128)(2,1)} %reshape.158), calls=%async_computation.1 | async-start | bytes 2097152 | tf_op jit(solution)/shard_map/all_to_all | solution.py:43
  214.8 1.2 copy-start
Sparse Core Ops, SparseCore 0:
  29.1 124.7 all-gather.1
where the time goes:
time: 225 us
  waiting for transfers between devices  135 us (60%)
  local copies, waits for them, and re-layouts  24 us (11%)
  blocking collectives  18.5 us (8%)
  between operations  17.5 us (8%)
  matrix products  12.5 us (6%)
  other arithmetic  10.9 us (5%)
  starting transfers between devices  6.33 us (3%)
    all_gather x1, waiting for transfers between devices, per_device(): lax.all_gather(amps_vm, 'pair', axis=0, tiled=True)  111 us
    all_to_all x1, waiting for transfers between devices, per_device(): lax.all_to_all(outgoing.astype(jnp.bfloat16), ('pair', 'virt'), split_axi...  24.5 us
    all_to_all x1, blocking collectives, per_device(): lax.all_to_all(amps_pm, 'virt', split_axis=1, concat_axis=0, tiled=True)  18.5 us
    convert_element_type x2, other arithmetic, per_device(): outgoing.astype(jnp.bfloat16)  10.9 us
    dot_general x1, matrix products, per_device(): jnp.einsum('rkc,kco->rko', chosen, integrals, preferred_element_type=jnp....  9.16 us
    unnamed x12, local copies, waits for them, and re-layouts  7.49 us
  transfers between devices with their start and end apart: 3, of which 2 were waited for; matrix products, arithmetic and copies ran while one was open for 17% of the time, Pallas kernels for 0%

commit v1 on v0

--- a/solution.py
+++ b/solution.py
@@ -7,6 +7,17 @@
 NVT = 8
 A_W = 8
 AS = 32
+
+
+def cut_along(value, dim, size):
+    before, after = (value.shape[:dim], value.shape[dim + 1 :])
+    return jnp.moveaxis(value.reshape(*before, size, -1, *after), dim, 0)
+
+
+def laid_out(tiles, dim):
+    tiles = jnp.moveaxis(tiles, 0, dim)
+    dims = tiles.shape
+    return tiles.reshape(*dims[:dim], dims[dim] * dims[dim + 1], *dims[dim + 2 :])
 
 
 def per_device(amps_pm, integrals, fock_vv, blk_tiles, blk_mask):
@@ -21,7 +32,14 @@
     own_tiles = lax.dynamic_slice_in_dim(blk_tiles, device * blk_dev, blk_dev, 0)
     own_mask = lax.dynamic_slice_in_dim(blk_mask, device * blk_dev, blk_dev, 0).astype(jnp.float32)
     local_in = own_tiles[:, 0] - virt_idx * slab
-    amps_vm = lax.all_to_all(amps_pm, "virt", split_axis=1, concat_axis=0, tiled=True)
+    peers, place = (lax.axis_size("virt"), lax.axis_index("virt"))
+    parts = cut_along(amps_pm, 1, peers)
+    outs = [parts[place]]
+    for turn in range(1, peers):
+        sent = parts[place ^ turn]
+        outs.append(lax.ppermute(sent, "virt", [(i, i ^ turn) for i in range(peers)]))
+    parts = jnp.stack(outs)[place ^ jnp.arange(peers)]
+    amps_vm = laid_out(parts, 0)
     sub_rows = amps_pm[:, :, :out_cols].reshape(pm_rows, A_W, NVT, AS, TILE)
     fock_four = fock_vv.reshape(NVT, TILE, NVT, TILE)
     onebody = jnp.einsum(

time: 225 us -> 218 us (0.969)
  blocking collectives: 18.5 us -> 0 us
  waiting for transfers between devices: 135 us -> 148 us
  local copies, waits for them, and re-layouts: 24 us -> 20 us
  starting transfers between devices: 6.33 us -> 9.52 us
    all_to_all x1 -> x0, blocking collectives: 18.5 us -> none  [per_device(): lax.all_to_all(amps_pm, 'virt', split_axis=1, concat_axis=0, tiled=True)]
    ppermute x0 -> x3, waiting for transfers between devices: none -> 11 us  [per_device(): lax.ppermute(sent, 'virt', [(i, i ^ turn) for i in range(peers)])]
    another operation x1 -> x0, local copies, waits for them, and re-layouts: 3.53 us -> none  [per_device(): jnp.take(lax.all_gather(amps_vm, 'pair', axis=0, tiled=True), local_in, a...]
    ppermute x0 -> x3, starting transfers between devices: none -> 3.23 us  [per_device(): lax.ppermute(sent, 'virt', [(i, i ^ turn) for i in range(peers)])]
    unnamed x12 -> x13, local copies, waits for them, and re-layouts: 7.49 us -> 5.21 us
  transfers between devices with their start and end apart: 3 -> 6, of which waited for: 2 -> 4; matrix products, arithmetic and copies ran while one was open for 17% -> 16% of each run, Pallas kernels for 0% -> 0%
where the time goes in v1:
time: 218 us
  waiting for transfers between devices  148 us (68%)
  local copies, waits for them, and re-layouts  20 us (9%)
  between operations  17.5 us (8%)
  matrix products  12.3 us (6%)
  other arithmetic  11.1 us (5%)
  starting transfers between devices  9.52 us (4%)
    all_gather x1, waiting for transfers between devices, per_device(): lax.all_gather(amps_vm, 'pair', axis=0, tiled=True)  112 us
    all_to_all x1, waiting for transfers between devices, per_device(): lax.all_to_all(outgoing.astype(jnp.bfloat16), ('pair', 'virt'), split_axi...  24.5 us
    ppermute x3, waiting for transfers between devices, per_device(): lax.ppermute(sent, 'virt', [(i, i ^ turn) for i in range(peers)])  11 us
    convert_element_type x2, other arithmetic, per_device(): outgoing.astype(jnp.bfloat16)  10.9 us
    dot_general x1, matrix products, per_device(): jnp.einsum('rkc,kco->rko', chosen, integrals, preferred_element_type=jnp....  8.97 us
    unnamed x13, local copies, waits for them, and re-layouts  5.21 us
  transfers between devices with their start and end apart: 6, of which 4 were waited for; matrix products, arithmetic and copies ran while one was open for 16% of the time, Pallas kernels for 0%

profile of v1, /device:TPU:0, one launch (start us, length us, event | category | flops | bytes accessed | tf_op | source)
XLA Modules:
  0.0 217.9 jit_solution(5115919389593163842)
XLA Ops:
  6.5 1.3 dynamic-slice_bitcast_fusion.3
  7.8 3.0 %collective-permute-start.1 = (bf16[2,16,4096]{2,1,0:T(8,128)(2,1)S(1)}, bf16[2,16,4096]{2,1,0:T(8,128)(2,1)S(1)}, u32[]{:S(2)}, u32[]{:S(2)}) collective-permute-start(bf16[2,16,4096]{2,1,0:T(8,128)(2,1)S(1)} %get-tuple-element.17), channel_id=1, source_target_pairs={{0,2},{1,3},{2,0},{3,1},{4,6},{5,7},{6,4},{7,5},{8,10},{9,11},{10,... | collective-permute-start | bytes 786440 | tf_op jit(solution)/shard_map/ppermute | solution.py:40
  10.8 0.2 collective-permute-start
  11.1 6.9 %collective-permute-done.1 = bf16[2,16,4096]{2,1,0:T(8,128)(2,1)S(1)} collective-permute-done((bf16[2,16,4096]{2,1,0:T(8,128)(2,1)S(1)}, bf16[2,16,4096]{2,1,0:T(8,128)(2,1)S(1)}, u32[]{:S(2)}, u32[]{:S(2)}) %collective-permute-start.1) | collective-permute-done | bytes 262176 | tf_op jit(solution)/shard_map/ppermute | solution.py:40
  18.0 4.0 %collective-permute-done.2 = bf16[2,16,4096]{2,1,0:T(8,128)(2,1)S(1)} collective-permute-done((bf16[2,16,4096]{2,1,0:T(8,128)(2,1)S(1)}, bf16[2,16,4096]{2,1,0:T(8,128)(2,1)S(1)}, u32[]{:S(2)}, u32[]{:S(2)}) %collective-permute-start.2) | collective-permute-done | bytes 262176 | tf_op jit(solution)/shard_map/ppermute | solution.py:40
  22.0 0.1 pad_maximum_fusion
  22.2 0.6 gather_fusion
  22.8 1.5 copy.24
  24.4 1.1 reshape.193
  25.5 0.5 reshape.142
  26.1 1.3 convolution_bitcast_fusion.1
  27.3 0.2 copy.35
  27.6 2.1 reshape.196
  29.7 3.5 %all-to-all-start.1 = ((f32[2,64,2048]{2,0,1:T(2,128)}), f32[2,64,2048]{2,0,1:T(2,128)S(1)}, u32[]{:S(2)}, u32[]{:S(2)}) async-start(f32[2,64,2048]{2,0,1:T(2,128)} %reshape.196), calls=%async_computation.1 | async-start | bytes 2097152 | tf_op jit(solution)/shard_map/all_to_all | solution.py:49
  33.3 0.6 fusion.25
  36.5 0.6 dynamic_slice.14
  38.6 112.1 %all-gather.2.cloned.1.call-done = bf16[64,16,4096]{2,0,1:T(8,128)(2,1)} async-done(((bf16[8,16,4096]{2,0,1:T(8,128)(2,1)}), bf16[64,16,4096]{2,0,1:T(8,128)(2,1)}) %all-gather.2.cloned.1.call-update) | async-done | bytes 8388624 | tf_op jit(solution)/shard_map/all_gather | solution.py:50
  150.7 9.0 %fusion.7 = f32[8,8,2048]{2,1,0:T(8,128)S(1)} fusion(bf16[1,4096,2048]{2,1,0:T(8,128)(2,1)} %param.6, bf16[64,16,4096]{2,0,1:T(8,128)(2,1)} %all-gather.2.cloned.1.call-done, s32[]{:T(128)} %bitcast.15, pred[]{:T(512)} %bitcast.4, f32[]{:T(128)} %bitcast.18), kind=kOutput, calls=%fused_computation.7 | convolution fusion | flops 1074135040 | bytes 17827328 | tf_op jit(solution)/shard_map/rkc,kco->rko/dot_general | solution.py:51
  159.7 0.2 mul.66
  159.9 3.5 %mul.67 = f32[256,1,2048]{2,1,0:T(1,128)} reshape(f32[8,4,8,2048]{3,2,1,0:T(8,128)S(1)} %mul.66) | data formatting | bytes 4194304 | tf_op jit(solution)/shard_map/mul | solution.py:58
  163.4 3.1 %multiply_convert_fusion = bf16[256,1,2048]{2,1,0:T(2,128)(2,1)S(1)} fusion(f32[256,1,2048]{2,1,0:T(1,128)} %mul.67, f32[256]{0:T(256)S(1)} %mul.69), kind=kLoop, calls=%fused_computation.8 | loop fusion | flops 1048576 | bytes 3146752 | tf_op jit(solution)/shard_map/convert_element_type | solution.py:62
  166.6 0.5 broadcast.145
  167.1 7.8 %reduce = bf16[256,2048]{1,0:T(8,128)(2,1)} reduce(bf16[256,1,2048]{2,1,0:T(2,128)(2,1)S(1)} %multiply_convert_fusion, bf16[]{:T(256)} %broadcast.145), dimensions={1}, to_apply=%multiply_convert_fusion.reduce_sub_computation | reduce | bytes 2097154 | tf_op jit(solution)/shard_map/convert_element_type | solution.py:62
  174.9 2.9 %reshape.197 = bf16[32,2,8192]{2,1,0:T(2,128)(2,1)} reshape(bf16[256,2048]{1,0:T(8,128)(2,1)} %reduce) | data formatting | bytes 2097152
  177.8 2.8 %all-to-all-start = ((bf16[32,2,8192]{2,1,0:T(2,128)(2,1)}), bf16[32,2,8192]{2,1,0:T(2,128)(2,1)S(1)}, u32[]{:S(2)}, u32[]{:S(2)}) async-start(bf16[32,2,8192]{2,1,0:T(2,128)(2,1)} %reshape.197), calls=%async_computation | async-start | bytes 2097152 | tf_op jit(solution)/shard_map/all_to_all | solution.py:61
  180.6 0.6 copy.29
  181.2 1.1 copy.30
  182.3 24.5 %all-to-all-done = bf16[32,2,8192]{2,1,0:T(2,128)(2,1)S(1)} async-done(((bf16[32,2,8192]{2,1,0:T(2,128)(2,1)}), bf16[32,2,8192]{2,1,0:T(2,128)(2,1)S(1)}, u32[]{:S(2)}, u32[]{:S(2)}) %all-to-all-start) | async-done | bytes 1048608 | tf_op jit(solution)/shard_map/all_to_all | solution.py:61
  206.8 1.0 reshape.198
  207.8 0.6 copy.49
  208.5 0.6 copy-done
  209.1 2.0 fusion.3
  (23 shorter events, 0.4 us)
Async XLA Ops:
  6.5 144.2 %all-gather.2.cloned.1.call-start = ((), (), s32[]{:S(2)}) async-start(), calls=%async_computation.2 | async-start | bytes 9437184 | tf_op jit(solution)/shard_map/all_gather | solution.py:50
  7.8 10.2 %collective-permute-start.1 = (bf16[2,16,4096]{2,1,0:T(8,128)(2,1)S(1)}, bf16[2,16,4096]{2,1,0:T(8,128)(2,1)S(1)}, u32[]{:S(2)}, u32[]{:S(2)}) collective-permute-start(bf16[2,16,4096]{2,1,0:T(8,128)(2,1)S(1)} %get-tuple-element.17), channel_id=1, source_target_pairs={{0,2},{1,3},{2,0},{3,1},{4,6},{5,7},{6,4},{7,5},{8,10},{9,11},{10,... | collective-permute-start | bytes 786440 | tf_op jit(solution)/shard_map/ppermute | solution.py:40
  10.8 11.2 %collective-permute-start.2 = (bf16[2,16,4096]{2,1,0:T(8,128)(2,1)S(1)}, bf16[2,16,4096]{2,1,0:T(8,128)(2,1)S(1)}, u32[]{:S(2)}, u32[]{:S(2)}) collective-permute-start(bf16[2,16,4096]{2,1,0:T(8,128)(2,1)S(1)} %get-tuple-element.19), channel_id=1, source_target_pairs={{0,3},{1,2},{2,1},{3,0},{4,7},{5,6},{6,5},{7,4},{8,11},{9,10},{10,... | collective-permute-start | bytes 786440 | tf_op jit(solution)/shard_map/ppermute | solution.py:40
  10.8 11.2 %collective-permute-start = (bf16[2,16,4096]{2,1,0:T(8,128)(2,1)S(1)}, bf16[2,16,4096]{2,1,0:T(8,128)(2,1)S(1)}, u32[]{:S(2)}, u32[]{:S(2)}) collective-permute-start(bf16[2,16,4096]{2,1,0:T(8,128)(2,1)S(1)} %get-tuple-element.18), channel_id=1, source_target_pairs={{0,1},{1,0},{2,3},{3,2},{4,5},{5,4},{6,7},{7,6},{8,9},{9,8},{10,11... | collective-permute-start | bytes 786440 | tf_op jit(solution)/shard_map/ppermute | solution.py:40
  22.8 1.6 copy-start.1
  24.3 1.2 copy-start.2
  27.5 5.7 %copy-start.3 = (s32[32,2]{0,1:T(2,128)S(1)}, s32[32,2]{0,1:T(2,128)}, u32[]{:S(2)}) copy-start(s32[32,2]{0,1:T(2,128)} %param.8) | copy-start | bytes 772
  27.6 8.9 %copy-start.4 = (s32[32]{0:T(128)S(1)}, s32[32]{0:T(128)}, u32[]{:S(2)}) copy-start(s32[32]{0:T(128)} %param.9) | copy-start | bytes 388
  29.7 148.1 %all-to-all-start.1 = ((f32[2,64,2048]{2,0,1:T(2,128)}), f32[2,64,2048]{2,0,1:T(2,128)S(1)}, u32[]{:S(2)}, u32[]{:S(2)}) async-start(f32[2,64,2048]{2,0,1:T(2,128)} %reshape.196), calls=%async_computation.1 | async-start | bytes 2097152 | tf_op jit(solution)/shard_map/all_to_all | solution.py:49
  177.8 29.0 %all-to-all-start = ((bf16[32,2,8192]{2,1,0:T(2,128)(2,1)}), bf16[32,2,8192]{2,1,0:T(2,128)(2,1)S(1)}, u32[]{:S(2)}, u32[]{:S(2)}) async-start(bf16[32,2,8192]{2,1,0:T(2,128)(2,1)} %reshape.197), calls=%async_computation | async-start | bytes 2097152 | tf_op jit(solution)/shard_map/all_to_all | solution.py:61
  207.8 1.2 copy-start
Sparse Core Ops, SparseCore 0:
  24.5 126.1 all-gather.1
